TPU v7x, 512 devices: a whole 4x8x8 slice. The times are simulated.
512 devices in a mesh: seq: 32 (over x, y), row: 4 (over z_hi, core), col: 4 (over z_lo).
Axes of the slice: x: 4, y: 8, z: 8 (z_hi: 2, z_lo: 4; z = z_hi * 4 + z_lo), core: 2. Of those that a mesh axis runs over, the one named last changes fastest.
Arguments:
- queries: bfloat16 [2048, 8192], P(('seq', 'row', 'col')), may hold values from -6 to 6
- new_keys: bfloat16 [2048, 1024], P(('seq', 'row', 'col')), may hold values from -6 to 6
- new_values: bfloat16 [2048, 1024], P(('seq', 'row', 'col')), may hold values from -6 to 6
- positions: int32 [2048], P(('seq', 'row', 'col')), may hold values from 0 to 2047, each once
- cache_keys: bfloat16 [4096, 1024], P(('row', 'col')), may hold values from -6 to 6
- cache_values: bfloat16 [4096, 1024], P(('row', 'col')), may hold values from -6 to 6
- slab_start: int32 [1], replicated, may hold values from 2048 to 4096
Outputs:
- context: bfloat16 [2048, 8192], P(('seq', 'row', 'col'))
Inputs may be any that keep to these rules, and one draw needn't show every extreme that they name: positions holds every number of 0 to 2047 once.
All inputs are finite; a program needn't handle non-finite values.
Results may differ from a plain program's by a relative error of at most 0.0065.
Values may be sent and summed in bfloat16 or wider, within the bound.
No kernel may reach another device: no remote copies, remote signals or barrier semaphores. Data moves between devices by JAX's collectives and lax.ppermute only.
A program may use at most 64 MiB of HBM per device.

v0:
```python
import math
import jax
import jax.numpy as jnp
from jax import lax
from jax.sharding import PartitionSpec as P

HQ = 64
KVH = 8
HD = 128
far_position = 1073741824
masked_score = -1e30


def attend(carried, query_block, query_pos, key_rows, value_rows, key_pos, kv_dev):
    running_max, running_sum, running_out = carried
    key_count = key_rows.shape[0]
    head_size = query_block.shape[-1]
    score_scale = 1.0 / math.sqrt(head_size)
    block_size = 1024
    for offset in range(0, key_count, block_size):
        finish = min(key_count, offset + block_size)
        key_block = key_rows[offset:finish].reshape(finish - offset, kv_dev, head_size)
        value_block = value_rows[offset:finish].reshape(finish - offset, kv_dev, head_size)
        scores = (
            jnp.einsum("qghd,ngd->qghn", query_block, key_block, preferred_element_type=jnp.float32)
            * score_scale
        )
        allowed = (key_pos[offset:finish][None, :] <= query_pos[:, None])[:, None, None, :]
        updated = jnp.maximum(
            running_max, jnp.max(jnp.where(allowed, scores, masked_score), axis=-1)
        )
        exponent = jnp.where(allowed, jnp.exp(scores - updated[..., None]), 0.0)
        factor = jnp.exp(running_max - updated)
        running_sum = running_sum * factor + jnp.sum(exponent, axis=-1)
        running_out = running_out * factor[..., None] + jnp.einsum(
            "qghn,ngd->qghd",
            exponent.astype(jnp.bfloat16),
            value_block,
            preferred_element_type=jnp.float32,
        )
        running_max = updated
    return (running_max, running_sum, running_out)


def spread_heads(matrix, seq_count, kv_dev, head_size):
    row_count = matrix.shape[0]
    kv_heads = matrix.shape[1] // head_size
    repeat = max(1, seq_count * kv_dev // kv_heads)
    reshaped = matrix.reshape(row_count, kv_heads, head_size)
    reshaped = jnp.repeat(reshaped, repeat, axis=1)
    return reshaped


def on_device(queries, new_keys, new_values, positions, cache_keys, cache_values, slab_start):
    seq_count = lax.axis_size("seq")
    cell_count = lax.axis_size("row") * lax.axis_size("col")
    cell_index = lax.axis_index("row") * lax.axis_size("col") + lax.axis_index("col")
    heads_dev = HQ // seq_count
    group_size = HQ // KVH
    kv_dev = max(1, heads_dev // group_size)
    per_group = heads_dev // kv_dev
    tok_rows = queries.shape[0]
    first_pos = slab_start[0]
    kv_first = lax.axis_index("seq") * heads_dev // group_size
    every_pos = lax.all_gather(positions, ("seq", "row", "col"), axis=0, tiled=True)
    regrouped = lax.all_to_all(queries, "seq", split_axis=1, concat_axis=0, tiled=True)
    query_count = regrouped.shape[0]
    query_block = regrouped.reshape(query_count, kv_dev, per_group, HD)
    own_pos = (
        lax.dynamic_index_in_dim(
            every_pos.reshape(seq_count, cell_count, tok_rows), cell_index, 1, keepdims=False
        ).reshape(query_count)
        + first_pos
    )
    cache_key_head = lax.dynamic_slice_in_dim(cache_keys, kv_first * HD, kv_dev * HD, 1)
    cache_value_head = lax.dynamic_slice_in_dim(cache_values, kv_first * HD, kv_dev * HD, 1)
    carried = (
        jnp.full((query_count, kv_dev, per_group), masked_score, jnp.float32),
        jnp.zeros((query_count, kv_dev, per_group), jnp.float32),
        jnp.zeros((query_count, kv_dev, per_group, HD), jnp.float32),
    )
    grouped = (
        lax.all_gather(new_keys, ("row", "col"), axis=0, tiled=True),
        lax.all_gather(new_values, ("row", "col"), axis=0, tiled=True),
    )
    received = (
        lax.all_to_all(
            spread_heads(grouped[0], seq_count, kv_dev, HD),
            "seq",
            split_axis=1,
            concat_axis=0,
            tiled=True,
        ),
        lax.all_to_all(
            spread_heads(grouped[1], seq_count, kv_dev, HD),
            "seq",
            split_axis=1,
            concat_axis=0,
            tiled=True,
        ),
    )
    slab_keys = received[0].reshape(-1, kv_dev * HD)
    slab_values = received[1].reshape(-1, kv_dev * HD)
    carried = attend(
        carried, query_block, own_pos, slab_keys, slab_values, every_pos + first_pos, kv_dev
    )
    pieces = (
        lax.all_gather(cache_key_head, ("row", "col"), axis=0, tiled=True),
        lax.all_gather(cache_value_head, ("row", "col"), axis=0, tiled=True),
    )
    row_ids = jnp.arange(pieces[0].shape[0], dtype=jnp.int32)
    key_pos = jnp.where(row_ids < first_pos, row_ids, far_position)
    carried = attend(carried, query_block, own_pos, pieces[0], pieces[1], key_pos, kv_dev)
    running_max, running_sum, running_out = carried
    context = (
        (running_out / running_sum[..., None])
        .astype(jnp.bfloat16)
        .reshape(query_count, heads_dev * HD)
    )
    return lax.all_to_all(context, "seq", split_axis=0, concat_axis=1, tiled=True)


def solution(mesh):
    in_specs = (
        P(("seq", "row", "col"), None),
        P(("seq", "row", "col"), None),
        P(("seq", "row", "col"), None),
        P(("seq", "row", "col")),
        P(("row", "col"), None),
        P(("row", "col"), None),
        P(),
    )
    out_specs = P(("seq", "row", "col"), None)
    return jax.shard_map(
        on_device, mesh=mesh, in_specs=in_specs, out_specs=out_specs, check_vma=False
    )
```

profile of v0, /device:TPU:1, one launch (start us, length us, event | category | flops | bytes accessed | tf_op | source)
XLA Modules:
  0.0 255.7 jit_solution(11486921465186553433)
XLA Ops:
  6.5 0.0 copy-start
  6.5 0.0 all-gather.5.cloned.1.call-start
  6.5 1.0 copy-done
  7.6 0.6 constant_dynamic-slice_fusion.1
  8.2 0.0 all-gather.5.cloned.1.call-update
  8.2 0.0 copy-start.12
  8.3 10.5 %all-to-all-start.1 = ((bf16[4,32,256]{2,0,1:T(4,128)(2,1)}), bf16[4,32,256]{2,0,1:T(4,128)(2,1)S(1)}, u32[]{:S(2)}, u32[]{:S(2)}) async-start(bf16[4,32,256]{2,0,1:T(4,128)(2,1)} %bitcast.7), calls=%async_computation.1 | async-start | bytes 131072 | tf_op jit(solution)/shard_map/all_to_all | solution.py:66
  18.8 33.7 %all-gather = bf16[16,4,1024]{2,1,0:T(4,128)(2,1)S(1)} all-gather(bf16[1,4,1024]{2,1,0:T(4,128)(2,1)S(1)} %bitcast.165), channel_id=1, replica_groups=mesh['seq'=32,'row'=4,'col'=4] {'row','col'}, dimensions={0}, use_global_device_ids=true | all-gather | bytes 139264 | tf_op jit(solution)/shard_map/all_gather | solution.py:83
  52.5 0.1 reshape.574
  52.6 0.0 all-to-all-done.1
  52.6 0.9 broadcast_in_dim.118
  53.5 8.9 %all-to-all-start = ((bf16[64,32,128]{2,0,1:T(8,128)(2,1)}), bf16[64,32,128]{2,0,1:T(8,128)(2,1)S(1)}, u32[]{:S(2)}, u32[]{:S(2)}) async-start(bf16[64,32,128]{2,0,1:T(8,128)(2,1)} %bitcast.2), calls=%async_computation | async-start | bytes 1048576 | tf_op jit(solution)/shard_map/all_to_all | solution.py:87
  62.4 0.0 all-gather.7.cloned.1.call-start
  62.5 0.9 constant_dynamic-slice_fusion
  63.3 0.7 copy.73
  64.1 0.0 all-gather.7.cloned.1.call-update
  64.1 0.0 copy-start.16
  64.1 0.6 copy-done.16
  64.8 0.2 dynamic-update-slice
  64.9 99.9 %all-reduce = s32[2048]{0:T(1024)S(1)} all-reduce(s32[2048]{0:T(1024)S(1)} %dynamic-update-slice), channel_id=1, replica_groups=mesh['seq'=32,'row'=4,'col'=4] {'seq','row','col'}, use_global_device_ids=true, to_apply=%add | all-reduce | flops 2048 | bytes 16384
  164.8 0.3 reshape.573
  165.8 0.1 add_reduce_fusion
  165.8 0.0 copy-start.13
  165.8 0.1 add.111
  165.9 0.6 copy-done.13
  166.5 28.9 %all-gather.1 = bf16[16,4,1024]{2,1,0:T(4,128)(2,1)S(1)} all-gather(bf16[1,4,1024]{2,1,0:T(4,128)(2,1)S(1)} %bitcast.166), channel_id=1, replica_groups=mesh['seq'=32,'row'=4,'col'=4] {'row','col'}, dimensions={0}, use_global_device_ids=true | all-gather | bytes 139264 | tf_op jit(solution)/shard_map/all_gather | solution.py:84
  195.4 0.1 reshape.579
  195.5 0.0 all-to-all-done
  195.5 0.9 broadcast_in_dim.122
  196.4 7.4 %all-to-all-start.2 = ((bf16[64,32,128]{2,0,1:T(8,128)(2,1)}), bf16[64,32,128]{2,0,1:T(8,128)(2,1)S(1)}, u32[]{:S(2)}, u32[]{:S(2)}) async-start(bf16[64,32,128]{2,0,1:T(8,128)(2,1)} %bitcast.14), calls=%async_computation.2 | async-start | bytes 1048576 | tf_op jit(solution)/shard_map/all_to_all | solution.py:94
  203.8 2.1 broadcast_compare_fusion.5
  206.0 13.7 %all-to-all-done.2 = bf16[64,32,128]{2,0,1:T(8,128)(2,1)S(1)} async-done(((bf16[64,32,128]{2,0,1:T(8,128)(2,1)}), bf16[64,32,128]{2,0,1:T(8,128)(2,1)S(1)}, u32[]{:S(2)}, u32[]{:S(2)}) %all-to-all-start.2) | async-done | bytes 524320 | tf_op jit(solution)/shard_map/all_to_all | solution.py:94
  219.7 0.8 fusion.77
  220.6 0.3 select_reduce_fusion.5
  220.9 0.3 select_reduce_fusion.4
  221.3 0.0 all-gather.5.cloned.1.call-done
  221.3 0.0 copy-start.15
  221.3 0.0 copy-start.8
  221.3 1.4 select_reduce_fusion.1
  222.7 0.4 select_reduce_fusion.2
  223.1 0.7 copy-done.9
  223.8 0.3 select_reduce_fusion.3
  224.1 0.0 copy-start.7
  224.1 0.0 copy-start.11
  224.2 0.3 select_reduce_fusion
  224.5 0.0 copy-start.3
  224.5 0.7 copy-done.11
  225.3 1.1 convolution_bitcast_fusion.4
  226.3 0.4 fusion.20
  226.8 0.4 fusion.24
  227.2 0.0 copy-done.1
  227.2 0.4 fusion.28
  227.7 0.0 all-gather.7.cloned.1.call-done
  227.8 1.9 convolution_bitcast_fusion.3
  229.7 1.5 convolution_bitcast_fusion.2
  231.2 0.5 convolution_bitcast_fusion.1
  231.7 0.8 copy-done.4
  232.4 0.4 convolution_bitcast_fusion
  232.9 0.5 copy-done.10
  233.4 0.0 copy-done.17
  233.4 0.5 fusion.19
  233.9 0.1 copy.62
  234.1 14.1 %all_to_all.65 = bf16[32,4,256]{2,1,0:T(4,128)(2,1)S(1)} all-to-all(bf16[32,4,256]{2,1,0:T(4,128)(2,1)S(1)} %all_to_all.57), channel_id=1, replica_groups=mesh['seq'=32,'row'=4,'col'=4] {'seq'}, dimensions={0} | all-to-all | bytes 131072 | tf_op jit(solution)/shard_map/all_to_all | solution.py:120
  248.2 0.6 copy.101
  (30 shorter events, 0.3 us)
Async XLA Ops:
  6.5 1.0 copy-start
  6.5 214.7 %all-gather.5.cloned.1.call-start = ((), (), s32[]{:S(2)}) async-start(), calls=%async_computation.4 | async-start | bytes 1114112 | tf_op jit(solution)/shard_map/all_gather | solution.py:108
  8.2 10.5 %copy-start.12 = (bf16[4,1024]{1,0:T(4,128)(2,1)S(1)}, bf16[4,1024]{1,0:T(4,128)(2,1)}, u32[]{:S(2)}) copy-start(bf16[4,1024]{1,0:T(4,128)(2,1)} %param.8) | copy-start | bytes 24580
  8.3 44.3 %all-to-all-start.1 = ((bf16[4,32,256]{2,0,1:T(4,128)(2,1)}), bf16[4,32,256]{2,0,1:T(4,128)(2,1)S(1)}, u32[]{:S(2)}, u32[]{:S(2)}) async-start(bf16[4,32,256]{2,0,1:T(4,128)(2,1)} %bitcast.7), calls=%async_computation.1 | async-start | bytes 131072 | tf_op jit(solution)/shard_map/all_to_all | solution.py:66
  53.5 142.0 %all-to-all-start = ((bf16[64,32,128]{2,0,1:T(8,128)(2,1)}), bf16[64,32,128]{2,0,1:T(8,128)(2,1)S(1)}, u32[]{:S(2)}, u32[]{:S(2)}) async-start(bf16[64,32,128]{2,0,1:T(8,128)(2,1)} %bitcast.2), calls=%async_computation | async-start | bytes 1048576 | tf_op jit(solution)/shard_map/all_to_all | solution.py:87
  62.4 165.3 %all-gather.7.cloned.1.call-start = ((), (), s32[]{:S(2)}) async-start(), calls=%async_computation.5 | async-start | bytes 1114112 | tf_op jit(solution)/shard_map/all_gather | solution.py:109
  64.1 0.7 copy-start.16
  165.8 0.7 copy-start.13
  196.4 23.3 %all-to-all-start.2 = ((bf16[64,32,128]{2,0,1:T(8,128)(2,1)}), bf16[64,32,128]{2,0,1:T(8,128)(2,1)S(1)}, u32[]{:S(2)}, u32[]{:S(2)}) async-start(bf16[64,32,128]{2,0,1:T(8,128)(2,1)} %bitcast.14), calls=%async_computation.2 | async-start | bytes 1048576 | tf_op jit(solution)/shard_map/all_to_all | solution.py:94
  221.3 1.4 copy-start.15
  221.3 1.4 copy-start.8
  222.7 4.5 %copy-start.1 = (f32[128,1,2,1024]{0,3,2,1:T(8,128)}, f32[128,1,2,1024]{0,3,2,1:T(8,128)S(1)}, u32[]{:S(2)}) copy-start(f32[128,1,2,1024]{0,3,2,1:T(8,128)S(1)} %get-tuple-element.37) | copy-start | bytes 3145732
  222.7 1.1 copy-start.9
  223.1 3.7 %copy-start.5 = (f32[128,1,2,1024]{0,3,2,1:T(8,128)}, f32[128,1,2,1024]{0,3,2,1:T(8,128)S(1)}, u32[]{:S(2)}) copy-start(f32[128,1,2,1024]{0,3,2,1:T(8,128)S(1)} %get-tuple-element.39) | copy-start | bytes 3145732
  224.1 2.6 %copy-start.7 = (f32[128,1,2,1024]{0,3,2,1:T(8,128)}, f32[128,1,2,1024]{0,3,2,1:T(8,128)S(1)}, u32[]{:S(2)}) copy-start(f32[128,1,2,1024]{0,3,2,1:T(8,128)S(1)} %get-tuple-element.41) | copy-start | bytes 3145732
  224.1 1.1 copy-start.11
  224.5 2.7 %copy-start.3 = (f32[128,1,2,1024]{0,3,2,1:T(8,128)}, f32[128,1,2,1024]{0,3,2,1:T(8,128)S(1)}, u32[]{:S(2)}) copy-start(f32[128,1,2,1024]{0,3,2,1:T(8,128)S(1)} %get-tuple-element.35) | copy-start | bytes 3145732
  227.7 2.0 copy-start.6
  227.8 3.4 %copy-start.14 = (bf16[4096,128]{0,1:T(8,128)(2,1)S(1)}, bf16[4096,128]{0,1:T(8,128)(2,1)}, u32[]{:S(2)}) copy-start(bf16[4096,128]{0,1:T(8,128)(2,1)} %all-gather.7.cloned.1.call-done) | copy-start | bytes 3145732
  229.7 1.5 copy-start.2
  231.2 1.2 copy-start.4
  232.4 0.9 copy-start.10
  232.4 1.0 copy-start.17
Sparse Core Ops, SparseCore 0:
  9.4 71.4 all-gather.4
  82.9 63.6 all-gather.6
where the time goes:
time: 256 us
  blocking collectives  177 us (69%)
  starting transfers between devices  26.8 us (10%)
  between operations  14.5 us (6%)
  waiting for transfers between devices  13.8 us (5%)
  local copies, waits for them, and re-layouts  11.4 us (4%)
  matrix products  8.99 us (4%)
  other arithmetic  3.52 us (1%)
    unnamed x1, blocking collectives  99.9 us
    all_gather x1, blocking collectives, on_device(): lax.all_gather(new_keys, ('row', 'col'), axis=0, tiled=True)  33.7 us
    all_gather x1, blocking collectives, on_device(): lax.all_gather(new_values, ('row', 'col'), axis=0, tiled=True)  28.9 us
    all_to_all x1, blocking collectives, on_device(): lax.all_to_all(context, 'seq', split_axis=0, concat_axis=1, tiled=True)  14.1 us
    all_to_all x1, waiting for transfers between devices, on_device(): lax.all_to_all(spread_heads(grouped[1], seq_count, kv_dev, HD), 'seq', sp...  13.7 us
    all_to_all x1, starting transfers between devices, on_device(): lax.all_to_all(queries, 'seq', split_axis=1, concat_axis=0, tiled=True)  10.5 us
    all_to_all x1, starting transfers between devices, on_device(): lax.all_to_all(spread_heads(grouped[0], seq_count, kv_dev, HD), 'seq', sp...  8.93 us
    all_to_all x1, starting transfers between devices, on_device(): lax.all_to_all(spread_heads(grouped[1], seq_count, kv_dev, HD), 'seq', sp...  7.36 us
  transfers between devices with their start and end apart: 5, of which 1 were waited for; matrix products, arithmetic and copies ran while one was open for 5% of the time, Pallas kernels for 0%

commit v1 on v0

--- a/solution.py
+++ b/solution.py
@@ -79,8 +79,17 @@
         jnp.zeros((query_count, kv_dev, per_group), jnp.float32),
         jnp.zeros((query_count, kv_dev, per_group, HD), jnp.float32),
     )
+    _close_scales = lambda sheet, dim_at: jnp.concatenate(
+        lax.all_to_all(
+            jnp.stack([sheet for _ in range(lax.axis_size(("row", "col")))], axis=0),
+            ("row", "col"),
+            0,
+            0,
+        ),
+        axis=dim_at,
+    )
     grouped = (
-        lax.all_gather(new_keys, ("row", "col"), axis=0, tiled=True),
+        _close_scales(new_keys, 0),
         lax.all_gather(new_values, ("row", "col"), axis=0, tiled=True),
     )
     received = (

time: 256 us -> 240 us (0.938)
  blocking collectives: 177 us -> 165 us
  starting transfers between devices: 26.8 us -> 23.8 us
    all_gather x1 -> x0, blocking collectives: 33.7 us -> none  [on_device(): lax.all_gather(new_keys, ('row', 'col'), axis=0, tiled=True)]
    all_to_all x0 -> x1, blocking collectives: none -> 19.3 us  [on_device(): lax.all_to_all(queries, 'seq', split_axis=1, concat_axis=0, tiled=True)]
    all_to_all x1, waiting for transfers between devices: 13.7 us -> 0.01 us  [on_device(): lax.all_to_all(spread_heads(grouped[1], seq_count, kv_dev, HD), 'seq', sp...]
    all_to_all x1, waiting for transfers between devices: 0.01 us -> 12.2 us  [on_device(): lax.all_to_all(spread_heads(grouped[0], seq_count, kv_dev, HD), 'seq', sp...]
    all_to_all x1, starting transfers between devices: 7.36 us -> 3.89 us  [on_device(): lax.all_to_all(spread_heads(grouped[1], seq_count, kv_dev, HD), 'seq', sp...]
    unnamed x40 -> x38, local copies, waits for them, and re-layouts: 6.57 us -> 6.11 us
where the time goes in v1:
time: 240 us; the launch traced here: 239 us
  blocking collectives  165 us (69%)
  starting transfers between devices  23.8 us (10%)
  between operations  14.4 us (6%)
  waiting for transfers between devices  12.3 us (5%)
  local copies, waits for them, and re-layouts  11.7 us (5%)
  matrix products  8.98 us (4%)
  other arithmetic  2.59 us (1%)
    unnamed x1, blocking collectives  99.3 us
    all_gather x1, blocking collectives, on_device(): lax.all_gather(new_values, ('row', 'col'), axis=0, tiled=True)  30.1 us
    all_to_all x1, blocking collectives, on_device(): lax.all_to_all(queries, 'seq', split_axis=1, concat_axis=0, tiled=True)  19.3 us
    all_to_all x1, blocking collectives, on_device(): lax.all_to_all(context, 'seq', split_axis=0, concat_axis=1, tiled=True)  16.1 us
    all_to_all x1, starting transfers between devices, on_device(): lax.all_to_all(jnp.stack([sheet for _ in range(lax.axis_size(('row', 'col...  12.6 us
    all_to_all x1, waiting for transfers between devices, on_device(): lax.all_to_all(spread_heads(grouped[0], seq_count, kv_dev, HD), 'seq', sp...  12.2 us
    all_to_all x1, starting transfers between devices, on_device(): lax.all_to_all(spread_heads(grouped[0], seq_count, kv_dev, HD), 'seq', sp...  7.3 us
    unnamed x38, local copies, waits for them, and re-layouts  6.11 us
  transfers between devices with their start and end apart: 5, of which 1 were waited for; matrix products, arithmetic and copies ran while one was open for 5% of the time, Pallas kernels for 0%

profile of v1, /device:TPU:1, one launch (start us, length us, event | category | flops | bytes accessed | tf_op | source)
XLA Modules:
  0.0 238.6 jit_solution(7832758550726782475)
XLA Ops:
  6.5 0.0 copy-start
  6.5 0.0 all-gather.4.cloned.1.call-start
  6.5 1.0 copy-done
  7.6 0.6 constant_dynamic-slice_fusion.1
  8.2 0.0 all-gather.4.cloned.1.call-update
  8.3 0.8 copy-done.10
  9.1 19.3 %all_to_all.70 = bf16[4,32,256]{2,0,1:T(4,128)(2,1)S(1)} all-to-all(bf16[4,32,256]{2,0,1:T(4,128)(2,1)S(1)} %bitcast.164), channel_id=1, replica_groups=mesh['seq'=32,'row'=4,'col'=4] {'seq'}, dimensions={1} | all-to-all | bytes 131072 | tf_op jit(solution)/shard_map/all_to_all | solution.py:66
  28.3 0.0 copy-done.11
  28.3 0.7 stack.2
  29.0 12.6 %all-to-all-start = ((bf16[16,4,1024]{2,1,0:T(4,128)(2,1)}), bf16[16,4,1024]{2,1,0:T(4,128)(2,1)S(1)}, u32[]{:S(2)}, u32[]{:S(2)}) async-start(bf16[16,4,1024]{2,1,0:T(4,128)(2,1)} %stack.2), calls=%async_computation | async-start | bytes 262144 | tf_op jit(solution)/shard_map/all_to_all | solution.py:83
  41.6 0.0 copy-done.12
  41.6 30.1 %all-gather = bf16[16,4,1024]{2,1,0:T(4,128)(2,1)S(1)} all-gather(bf16[1,4,1024]{2,1,0:T(4,128)(2,1)S(1)} %bitcast.165), channel_id=1, replica_groups=mesh['seq'=32,'row'=4,'col'=4] {'row','col'}, dimensions={0}, use_global_device_ids=true | all-gather | bytes 139264 | tf_op jit(solution)/shard_map/all_gather | solution.py:93
  71.7 0.1 reshape.577
  71.7 0.0 all-to-all-done
  71.8 0.9 broadcast_in_dim.122
  72.7 3.9 %all-to-all-start.3 = ((bf16[64,32,128]{2,0,1:T(8,128)(2,1)}), bf16[64,32,128]{2,0,1:T(8,128)(2,1)S(1)}, u32[]{:S(2)}, u32[]{:S(2)}) async-start(bf16[64,32,128]{2,0,1:T(8,128)(2,1)} %bitcast.13), calls=%async_computation.3 | async-start | bytes 1048576 | tf_op jit(solution)/shard_map/all_to_all | solution.py:103
  76.6 0.0 all-gather.6.cloned.1.call-start
  76.6 0.9 constant_dynamic-slice_fusion
  77.5 0.7 copy.72
  78.2 0.0 all-gather.6.cloned.1.call-update
  78.2 0.0 copy-start.15
  78.3 0.6 copy-done.15
  78.9 0.2 dynamic-update-slice
  79.1 99.3 %all-reduce = s32[2048]{0:T(1024)S(1)} all-reduce(s32[2048]{0:T(1024)S(1)} %dynamic-update-slice), channel_id=1, replica_groups=mesh['seq'=32,'row'=4,'col'=4] {'seq','row','col'}, use_global_device_ids=true, to_apply=%add | all-reduce | flops 2048 | bytes 16384
  178.4 0.3 reshape.572
  179.3 0.1 add_reduce_fusion
  179.4 0.1 add.111
  179.5 0.1 reshape_reshape.3
  179.6 0.0 all-to-all-done.3
  179.6 0.9 broadcast_in_dim.118
  180.5 7.3 %all-to-all-start.1 = ((bf16[64,32,128]{2,0,1:T(8,128)(2,1)}), bf16[64,32,128]{2,0,1:T(8,128)(2,1)S(1)}, u32[]{:S(2)}, u32[]{:S(2)}) async-start(bf16[64,32,128]{2,0,1:T(8,128)(2,1)} %bitcast.1), calls=%async_computation.1 | async-start | bytes 1048576 | tf_op jit(solution)/shard_map/all_to_all | solution.py:96
  187.9 1.2 broadcast_compare_fusion.5
  189.1 0.9 fusion.77
  190.0 12.2 %all-to-all-done.1 = bf16[64,32,128]{2,0,1:T(8,128)(2,1)S(1)} async-done(((bf16[64,32,128]{2,0,1:T(8,128)(2,1)}), bf16[64,32,128]{2,0,1:T(8,128)(2,1)S(1)}, u32[]{:S(2)}, u32[]{:S(2)}) %all-to-all-start.1) | async-done | bytes 524320 | tf_op jit(solution)/shard_map/all_to_all | solution.py:96
  202.2 0.3 select_reduce_fusion.5
  202.5 0.3 select_reduce_fusion.4
  202.9 0.0 all-gather.4.cloned.1.call-done
  202.9 0.0 copy-start.14
  202.9 1.4 select_reduce_fusion.1
  204.3 0.0 copy-start.1
  204.3 0.0 copy-done.14
  204.3 0.3 select_reduce_fusion.2
  204.7 0.0 copy-start.5
  204.7 0.3 select_reduce_fusion.3
  205.1 0.3 select_reduce_fusion
  205.4 0.8 copy-done.9
  206.2 1.1 convolution_bitcast_fusion.4
  207.3 0.4 fusion.20
  207.7 0.4 fusion.24
  208.2 0.0 copy-done.3
  208.2 0.4 fusion.28
  208.7 0.0 all-gather.6.cloned.1.call-done
  208.7 0.0 copy-start.13
  208.7 1.9 convolution_bitcast_fusion.3
  210.6 1.5 convolution_bitcast_fusion.2
  212.1 0.5 convolution_bitcast_fusion.1
  212.6 0.8 copy-done.4
  213.4 0.4 convolution_bitcast_fusion
  213.8 0.5 copy-done.8
  214.3 0.0 copy-done.16
  214.3 0.5 fusion.19
  214.9 0.1 copy.61
  215.0 16.1 %all_to_all.71 = bf16[32,4,256]{2,1,0:T(4,128)(2,1)S(1)} all-to-all(bf16[32,4,256]{2,1,0:T(4,128)(2,1)S(1)} %all_to_all.61), channel_id=1, replica_groups=mesh['seq'=32,'row'=4,'col'=4] {'seq'}, dimensions={0} | all-to-all | bytes 131072 | tf_op jit(solution)/shard_map/all_to_all | solution.py:129
  231.1 0.6 copy.100
  (29 shorter events, 0.3 us)
Async XLA Ops:
  6.5 1.0 copy-start
  6.5 196.4 %all-gather.4.cloned.1.call-start = ((), (), s32[]{:S(2)}) async-start(), calls=%async_computation.5 | async-start | bytes 1114112 | tf_op jit(solution)/shard_map/all_gather | solution.py:117
  8.2 0.8 copy-start.10
  9.1 19.3 %copy-start.11 = (bf16[4,1024]{1,0:T(4,128)(2,1)S(1)}, bf16[4,1024]{1,0:T(4,128)(2,1)}, u32[]{:S(2)}) copy-start(bf16[4,1024]{1,0:T(4,128)(2,1)} %param.8) | copy-start | bytes 24580
  29.0 12.6 %copy-start.12 = (bf16[4,1024]{1,0:T(4,128)(2,1)S(1)}, bf16[4,1024]{1,0:T(4,128)(2,1)}, u32[]{:S(2)}) copy-start(bf16[4,1024]{1,0:T(4,128)(2,1)} %param.9) | copy-start | bytes 24580
  29.0 42.7 %all-to-all-start = ((bf16[16,4,1024]{2,1,0:T(4,128)(2,1)}), bf16[16,4,1024]{2,1,0:T(4,128)(2,1)S(1)}, u32[]{:S(2)}, u32[]{:S(2)}) async-start(bf16[16,4,1024]{2,1,0:T(4,128)(2,1)} %stack.2), calls=%async_computation | async-start | bytes 262144 | tf_op jit(solution)/shard_map/all_to_all | solution.py:83
  72.7 106.9 %all-to-all-start.3 = ((bf16[64,32,128]{2,0,1:T(8,128)(2,1)}), bf16[64,32,128]{2,0,1:T(8,128)(2,1)S(1)}, u32[]{:S(2)}, u32[]{:S(2)}) async-start(bf16[64,32,128]{2,0,1:T(8,128)(2,1)} %bitcast.13), calls=%async_computation.3 | async-start | bytes 1048576 | tf_op jit(solution)/shard_map/all_to_all | solution.py:103
  76.6 132.1 %all-gather.6.cloned.1.call-start = ((), (), s32[]{:S(2)}) async-start(), calls=%async_computation.6 | async-start | bytes 1114112 | tf_op jit(solution)/shard_map/all_gather | solution.py:118
  78.2 0.7 copy-start.15
  180.5 21.6 %all-to-all-start.1 = ((bf16[64,32,128]{2,0,1:T(8,128)(2,1)}), bf16[64,32,128]{2,0,1:T(8,128)(2,1)S(1)}, u32[]{:S(2)}, u32[]{:S(2)}) async-start(bf16[64,32,128]{2,0,1:T(8,128)(2,1)} %bitcast.1), calls=%async_computation.1 | async-start | bytes 1048576 | tf_op jit(solution)/shard_map/all_to_all | solution.py:96
  202.9 1.4 copy-start.14
  204.3 3.8 %copy-start.1 = (f32[128,1,2,1024]{0,3,2,1:T(8,128)}, f32[128,1,2,1024]{0,3,2,1:T(8,128)S(1)}, u32[]{:S(2)}) copy-start(f32[128,1,2,1024]{0,3,2,1:T(8,128)S(1)} %get-tuple-element.37) | copy-start | bytes 3145732
  204.7 3.0 %copy-start.5 = (f32[128,1,2,1024]{0,3,2,1:T(8,128)}, f32[128,1,2,1024]{0,3,2,1:T(8,128)S(1)}, u32[]{:S(2)}) copy-start(f32[128,1,2,1024]{0,3,2,1:T(8,128)S(1)} %get-tuple-element.39) | copy-start | bytes 3145732
  205.0 2.7 %copy-start.7 = (f32[128,1,2,1024]{0,3,2,1:T(8,128)}, f32[128,1,2,1024]{0,3,2,1:T(8,128)S(1)}, u32[]{:S(2)}) copy-start(f32[128,1,2,1024]{0,3,2,1:T(8,128)S(1)} %get-tuple-element.41) | copy-start | bytes 3145732
  205.1 1.1 copy-start.9
  205.4 2.8 %copy-start.3 = (f32[128,1,2,1024]{0,3,2,1:T(8,128)}, f32[128,1,2,1024]{0,3,2,1:T(8,128)S(1)}, u32[]{:S(2)}) copy-start(f32[128,1,2,1024]{0,3,2,1:T(8,128)S(1)} %get-tuple-element.35) | copy-start | bytes 3145732
  208.6 2.0 copy-start.6
  208.7 3.4 %copy-start.13 = (bf16[4096,128]{0,1:T(8,128)(2,1)S(1)}, bf16[4096,128]{0,1:T(8,128)(2,1)}, u32[]{:S(2)}) copy-start(bf16[4096,128]{0,1:T(8,128)(2,1)} %all-gather.6.cloned.1.call-done) | copy-start | bytes 3145732
  210.6 1.5 copy-start.2
  212.1 1.2 copy-start.4
  213.4 0.9 copy-start.8
  213.4 1.0 copy-start.16
Sparse Core Ops, SparseCore 0:
  9.4 71.7 all-gather.3
  83.2 65.3 all-gather.5
